TPU v7x, 256 devices: a whole 4x4x8 slice. The times are simulated.
256 devices in a mesh: nodes: 64 (over z, y, core), mp: 4 (over x).
Axes of the slice: x: 4, y: 4, z: 8, core: 2. Of those that a mesh axis runs over, the one named last changes fastest.
Arguments:
- event_feats: bfloat16 [65536, 512], P('nodes'), may hold values from -6 to 6
- event_owner: int32 [65536, 1], P('nodes'), may hold values from 0 to 63; in each aligned block of 1024 rows (0 to 1023, 1024 to 2047, ...) at most 32 rows name the same one
- event_slot: int32 [65536], P('nodes'), may hold values from 0 to 255
- memory: bfloat16 [16384, 1024], P('nodes'), may hold values from -6 to 6
- w_msg_event: bfloat16 [512, 2048], P(None, 'mp'), may hold values from -0.25 to 0.25
- w_msg_state: bfloat16 [1024, 2048], P(None, 'mp'), may hold values from -0.1875 to 0.1875
- b_msg: float32 [2048], P('mp'), may hold values from -3 to 3
- w_msg_out: bfloat16 [2048, 1024], P('mp'), may hold values from -0.125 to 0.125
- b_out: float32 [1024], replicated, may hold values from -3 to 3
- w_input: bfloat16 [3, 1024, 1024], P(None, None, 'mp'), may hold values from -0.1875 to 0.1875
- w_hidden: bfloat16 [3, 1024, 1024], P(None, None, 'mp'), may hold values from -0.1875 to 0.1875
- b_input: float32 [3, 1024], P(None, 'mp'), may hold values from -3 to 3
- b_hidden: float32 [3, 1024], P(None, 'mp'), may hold values from -3 to 3
- state_slots: int32 [4096, 32], P('nodes'), may hold values from 0 to 255
- neighbours: int32 [16384, 10], P('nodes'), may hold values from 0 to 2047
- query_slots: int32 [16384], P('nodes'), may hold values from 0 to 255
- w_neigh: bfloat16 [1024, 1024], P('mp'), may hold values from -0.1875 to 0.1875
- w_self: bfloat16 [1024, 1024], P('mp'), may hold values from -0.1875 to 0.1875
- b_embed: float32 [1024], replicated, may hold values from -3 to 3
Outputs:
- new_memory: bfloat16 [16384, 1024], P('nodes', 'mp')
- embedding: bfloat16 [16384, 1024], P(('nodes', 'mp'))
Inputs may be any that keep to these rules, and one draw needn't show every extreme that they name: `event_owner`: among the 1024 events of one block of events, at most 32 name the same owner, and in every draw some owner is named exactly 32 times by some block.
All inputs are finite; a program needn't handle non-finite values.
Results may differ from a plain program's by a relative error of at most 0.014.
Values may be sent and summed in bfloat16 or wider, within the bound.
No kernel may reach another device: no remote copies, remote signals or barrier semaphores. Data moves between devices by JAX's collectives and lax.ppermute only.
A program may use at most 64 MiB of HBM per device.

v0:
```python
import jax
import jax.numpy as jnp
from jax import lax
from jax.sharding import PartitionSpec as P

F32 = jnp.float32
BF16 = jnp.bfloat16


def one_hot(index, size, dtype=BF16):
    return (index[:, None] == lax.broadcasted_iota(jnp.int32, (1, size), 1)).astype(dtype)


def one_hot_t(index, size, dtype=BF16):
    return (lax.broadcasted_iota(jnp.int32, (size, 1), 0) == index[None, :]).astype(dtype)


def split_dot(x32, w):
    hi = x32.astype(BF16)
    lo = (x32 - hi.astype(F32)).astype(BF16)
    return jnp.dot(hi, w, preferred_element_type=F32) + jnp.dot(lo, w, preferred_element_type=F32)


def per_device(
    event_feats,
    event_owner,
    event_slot,
    memory,
    w_msg_event,
    w_msg_state,
    b_msg,
    w_msg_out,
    b_out,
    w_input,
    w_hidden,
    b_input,
    b_hidden,
    state_slots,
    neighbours,
    query_slots,
    w_neigh,
    w_self,
    b_embed,
):
    owner_count = lax.axis_size("nodes")
    share_count = lax.axis_size("mp")
    mp_index = lax.axis_index("mp")
    event_rows = event_feats.shape[0]
    mem_rows = memory.shape[0]
    mem_width = memory.shape[1]
    col_share = mem_width // share_count
    capacity = 2 * event_rows // owner_count
    send_rows = owner_count * capacity
    owner = event_owner[:, 0]
    match = owner[:, None] == lax.broadcasted_iota(jnp.int32, (1, owner_count), 1)
    earlier = (
        lax.broadcasted_iota(jnp.int32, (event_rows, event_rows), 1)
        < lax.broadcasted_iota(jnp.int32, (event_rows, event_rows), 0)
    ).astype(BF16)
    before = jnp.dot(earlier, match.astype(BF16), preferred_element_type=F32)
    place = jnp.sum(jnp.where(match, before, 0.0), axis=1).astype(jnp.int32)
    target = owner * capacity + place
    route = one_hot_t(target, send_rows)
    feat_buffer = jnp.dot(route, event_feats, preferred_element_type=F32).astype(BF16)
    slot_col = jnp.broadcast_to((event_slot + 1).astype(BF16)[:, None], (event_rows, 128))
    id_buffer = jnp.dot(route, slot_col, preferred_element_type=F32)[:, 0].astype(jnp.int32) - 1
    feat_buffer = feat_buffer.reshape(owner_count, capacity, event_feats.shape[1])
    id_buffer = id_buffer.reshape(owner_count, capacity)
    arrived = lax.all_to_all(feat_buffer, "nodes", split_axis=0, concat_axis=0, tiled=True)
    arrived_ids = lax.all_to_all(id_buffer, "nodes", split_axis=0, concat_axis=0, tiled=True)
    arrived = arrived.reshape(send_rows, event_feats.shape[1])
    arrived_ids = arrived_ids.reshape(send_rows)
    seg = one_hot_t(arrived_ids, mem_rows)
    seg_t = one_hot(arrived_ids, mem_rows)
    counts = jnp.sum(seg.astype(F32), axis=1)
    state_proj = jnp.dot(memory, w_msg_state, preferred_element_type=F32)
    sp_hi = state_proj.astype(BF16)
    sp_lo = (state_proj - sp_hi.astype(F32)).astype(BF16)
    gathered = jnp.dot(seg_t, sp_hi, preferred_element_type=F32) + jnp.dot(
        seg_t, sp_lo, preferred_element_type=F32
    )
    pre = jnp.dot(arrived, w_msg_event, preferred_element_type=F32) + gathered + b_msg
    hidden_msg = jax.nn.relu(pre).astype(BF16)
    hidden_sum = jnp.dot(seg, hidden_msg, preferred_element_type=F32)
    partial_total = split_dot(hidden_sum, w_msg_out)
    divisor = jnp.maximum(counts, 1.0)[:, None]
    msg_total = lax.psum(partial_total.astype(BF16), "mp").astype(F32)
    aggregate = (msg_total / divisor + b_out).astype(BF16)
    gates_in = (
        jnp.einsum("nd,gdc->gnc", aggregate, w_input, preferred_element_type=F32)
        + b_input[:, None, :]
    )
    gates_st = (
        jnp.einsum("nd,gdc->gnc", memory, w_hidden, preferred_element_type=F32)
        + b_hidden[:, None, :]
    )
    reset_gate = jax.nn.sigmoid(gates_in[0] + gates_st[0])
    update_gate = jax.nn.sigmoid(gates_in[1] + gates_st[1])
    candidate = jnp.tanh(gates_in[2] + reset_gate * gates_st[2])
    old_state = lax.dynamic_slice_in_dim(memory, mp_index * col_share, col_share, 1).astype(F32)
    updated = (1.0 - update_gate) * candidate + update_gate * old_state
    new_memory = jnp.where((counts > 0.0)[:, None], updated, old_state).astype(BF16)
    pick = one_hot(state_slots.reshape(-1), mem_rows)
    outgoing = jnp.dot(pick, new_memory, preferred_element_type=F32).astype(BF16)
    outgoing = outgoing.reshape(state_slots.shape[0], state_slots.shape[1], col_share)
    relayed = lax.all_to_all(outgoing, "nodes", split_axis=0, concat_axis=0, tiled=True)
    relayed = relayed.reshape(relayed.shape[0] * relayed.shape[1], col_share)
    recv_rows = relayed.shape[0]
    neigh_count = one_hot(neighbours[:, 0], recv_rows, F32)
    for k in range(1, neighbours.shape[1]):
        neigh_count = neigh_count + one_hot(neighbours[:, k], recv_rows, F32)
    neigh_total = jnp.dot(neigh_count.astype(BF16), relayed, preferred_element_type=F32)
    neigh_mean = (neigh_total / neighbours.shape[1]).astype(BF16)
    self_state = jnp.dot(
        one_hot(query_slots, mem_rows), new_memory, preferred_element_type=F32
    ).astype(BF16)
    summed = lax.psum_scatter(
        (
            jnp.dot(neigh_mean, w_neigh, preferred_element_type=F32)
            + jnp.dot(self_state, w_self, preferred_element_type=F32)
        ).astype(BF16),
        "mp",
        scatter_dimension=0,
        tiled=True,
    ).astype(F32)
    embedding = jax.nn.relu(summed + b_embed).astype(BF16)
    return (new_memory, embedding)


def solution(mesh):
    in_specs = (
        P("nodes", None),
        P("nodes", None),
        P("nodes"),
        P("nodes", None),
        P(None, "mp"),
        P(None, "mp"),
        P("mp"),
        P("mp", None),
        P(),
        P(None, None, "mp"),
        P(None, None, "mp"),
        P(None, "mp"),
        P(None, "mp"),
        P("nodes", None),
        P("nodes", None),
        P("nodes"),
        P("mp", None),
        P("mp", None),
        P(),
    )
    out_specs = (P("nodes", "mp"), P(("nodes", "mp"), None))
    return jax.shard_map(
        per_device, mesh=mesh, in_specs=in_specs, out_specs=out_specs, check_vma=False
    )
```

profile of v0, /device:TPU:8, one launch (start us, length us, event | category | flops | bytes accessed | tf_op | source)
XLA Modules:
  0.0 229.8 jit_solution(13765049817450807412)
XLA Ops:
  7.2 0.8 add_convert_fusion.4
  8.0 0.2 reshape.97
  8.2 1.4 fusion.17
  9.6 0.8 convert_add_fusion
  10.4 1.6 fusion.19
  11.9 0.7 sub.16
  12.6 12.1 %all-to-all-start = ((s32[64,1,32]{2,1,0:T(1,128)}), s32[64,1,32]{2,1,0:T(1,128)S(1)}, u32[]{:S(2)}, u32[]{:S(2)}) async-start(s32[64,1,32]{2,1,0:T(1,128)} %bitcast.1), calls=%async_computation | async-start | bytes 65536 | tf_op jit(solution)/shard_map/all_to_all | solution.py:70
  24.7 3.7 %fusion.5 = bf16[2048,512]{1,0:T(8,128)(2,1)} fusion(bf16[1024,512]{1,0:T(8,128)(2,1)S(1)} %copy-done.12, s32[1024]{0:T(1024)S(1)} %convert_add_fusion), kind=kOutput, calls=%fused_computation.8 | convolution fusion | flops 2150629376 | bytes 3149824 | tf_op jit(solution)/shard_map/dot_general | solution.py:64
  28.4 4.9 %all-to-all-done = s32[64,1,32]{2,1,0:T(1,128)S(1)} async-done(((s32[64,1,32]{2,1,0:T(1,128)}), s32[64,1,32]{2,1,0:T(1,128)S(1)}, u32[]{:S(2)}, u32[]{:S(2)}) %all-to-all-start) | async-done | bytes 8224 | tf_op jit(solution)/shard_map/all_to_all | solution.py:70
  33.3 6.5 %all-to-all-start.1 = ((bf16[64,32,512]{2,1,0:T(8,128)(2,1)}), bf16[64,32,512]{2,1,0:T(8,128)(2,1)}, u32[]{:S(2)}, u32[]{:S(2)}) async-start(bf16[64,32,512]{2,1,0:T(8,128)(2,1)} %bitcast.51), calls=%async_computation.1 | async-start | bytes 4194304 | tf_op jit(solution)/shard_map/all_to_all | solution.py:69
  39.8 0.2 all-reduce.2.cloned.1.call-start
  40.2 1.5 fusion.78
  41.7 2.5 %fusion.13 = f32[3,256,256]{2,1,0:T(8,128)} fusion(bf16[3,1024,256]{2,1,0:T(8,128)(2,1)S(1)} %copy-done, bf16[256,1024]{1,0:T(8,128)(2,1)} %param.22, f32[3,256]{1,0:T(4,128)S(1)} %copy-done.13), kind=kOutput, calls=%fused_computation.35 | convolution fusion | flops 402849792 | bytes 2886656 | tf_op jit(solution)/shard_map/nd,gdc->gnc/dot_general | solution.py:94
  44.3 0.5 broadcast.59
  44.8 0.7 reduce.7
  45.6 2.4 %fusion.8 = f32[2048,512]{1,0:T(8,128)} fusion(s32[2048]{0:T(1024)S(1)} %eq.239, f32[256,512]{1,0:T(8,128)S(1)} %fusion.78), kind=kOutput, calls=%fused_computation.25 | convolution fusion | flops 537526272 | bytes 4726784 | tf_op jit(solution)/shard_map/dot_general | solution.py:79
  48.0 43.1 %all-to-all-done.1 = bf16[64,32,512]{2,1,0:T(8,128)(2,1)} async-done(((bf16[64,32,512]{2,1,0:T(8,128)(2,1)}), bf16[64,32,512]{2,1,0:T(8,128)(2,1)}, u32[]{:S(2)}, u32[]{:S(2)}) %all-to-all-start.1) | async-done | bytes 2097184 | tf_op jit(solution)/shard_map/all_to_all | solution.py:69
  91.1 4.8 %fusion.77 = f32[2048,512]{1,0:T(8,128)} fusion(bf16[2048,512]{1,0:T(8,128)(2,1)} %bitcast.3, bf16[512,512]{1,0:T(8,128)(2,1)S(1)} %copy-done.5), kind=kOutput, calls=%fused_computation.104 | convolution fusion | flops 1073741824 | bytes 6815744 | tf_op jit(solution)/shard_map/dot_general | solution.py:82
  95.9 6.0 %fusion.9 = f32[256,512]{1,0:T(8,128)} fusion(s32[2048]{0:T(1024)S(1)} %eq.239, f32[2048,512]{1,0:T(8,128)} %fusion.77, f32[2048,512]{1,0:T(8,128)} %fusion.8, f32[512]{0:T(512)S(1)} %copy-done.16, f32[256,512]{1,0:T(8,128)S(1)} %fusion.78), kind=kOutput, calls=%fused_computation.28 | convolution fusion | flops 1080557568 | bytes 9447424 | tf_op jit(solution)/shard_map/dot_general | solution.py:84
  101.9 1.5 fusion.68
  103.5 1.2 fusion.11
  104.8 0.3 convert_reduce_fusion
  105.1 44.3 %all-reduce.2.cloned.1.call-done = bf16[256,1024]{1,0:T(8,128)(2,1)} async-done(((bf16[256,1024]{1,0:T(8,128)(2,1)}), bf16[256,1024]{1,0:T(8,128)(2,1)}) %all-reduce.2.cloned.1.call-update) | async-done | bytes 524304 | tf_op jit(solution)/shard_map/psum | solution.py:87
  149.4 2.2 fusion.14
  151.6 1.1 fusion.50
  152.8 1.5 convolution_convert_fusion
  154.3 10.6 %all-to-all-start.2 = ((bf16[64,32,256]{2,1,0:T(8,128)(2,1)}), bf16[64,32,256]{2,1,0:T(8,128)(2,1)S(1)}, u32[]{:S(2)}, u32[]{:S(2)}) async-start(bf16[64,32,256]{2,1,0:T(8,128)(2,1)} %bitcast.53), calls=%async_computation.2 | async-start | bytes 2097152 | tf_op jit(solution)/shard_map/all_to_all | solution.py:106
  164.9 28.7 %all-to-all-done.2 = bf16[64,32,256]{2,1,0:T(8,128)(2,1)S(1)} async-done(((bf16[64,32,256]{2,1,0:T(8,128)(2,1)}), bf16[64,32,256]{2,1,0:T(8,128)(2,1)S(1)}, u32[]{:S(2)}, u32[]{:S(2)}) %all-to-all-start.2) | async-done | bytes 1048608 | tf_op jit(solution)/shard_map/all_to_all | solution.py:106
  193.6 5.2 %fusion.18 = f32[256,1024]{1,0:T(8,128)} fusion(bf16[256,1024]{1,0:T(8,128)(2,1)} %param.35, bf16[2048,256]{1,0:T(8,128)(2,1)S(1)} %bitcast.52, s32[256]{0:T(256)S(1)} %bitcast.64, s32[256]{0:T(256)S(1)} %bitcast.65, s32[256]{0:T(256)S(1)} %bitcast.57, s32[256]{0:T(256)S(1)} %bitcast.58, s32[256]{0:T(256)S(1)} %bitcast.59, s32[256]{0:T(256)S(1)} %bitcast.60, ...), kind=kOutput, calls=%fused_computation.43 | convolution fusion | flops 418512896 | bytes 2631680 | tf_op jit(solution)/shard_map/dot_general | solution.py:119
  198.9 2.5 %fusion.12 = bf16[256,1024]{1,0:T(8,128)(2,1)} fusion(f32[256,1024]{1,0:T(8,128)} %fusion.18, bf16[256,1024]{1,0:T(8,128)(2,1)S(1)} %copy-done.7, bf16[256,256]{1,0:T(8,128)(2,1)S(1)} %fusion.50, s32[256]{0:T(256)S(1)} %copy-done.11), kind=kOutput, calls=%fused_computation.33 | convolution fusion | flops 168427520 | bytes 2229248 | tf_op jit(solution)/shard_map/dot_general | solution.py:120
  201.4 20.0 %reduce-scatter.2.cloned.1.call-done = bf16[64,1024]{1,0:T(8,128)(2,1)} async-done(((bf16[256,1024]{1,0:T(8,128)(2,1)}), bf16[64,1024]{1,0:T(8,128)(2,1)}) %reduce-scatter.2.cloned.1.call-update) | async-done | bytes 131088 | tf_op jit(solution)/shard_map/reduce_scatter | solution.py:117
  221.4 1.6 maximum_convert_fusion.1
  (43 shorter events, 0.4 us)
Async XLA Ops:
  7.2 34.6 %copy-start = (bf16[3,1024,256]{2,1,0:T(8,128)(2,1)S(1)}, bf16[3,1024,256]{2,1,0:T(8,128)(2,1)}, u32[]{:S(2)}) copy-start(bf16[3,1024,256]{2,1,0:T(8,128)(2,1)} %param.29) | copy-start | bytes 4718596
  9.6 15.2 %copy-start.12 = (bf16[1024,512]{1,0:T(8,128)(2,1)S(1)}, bf16[1024,512]{1,0:T(8,128)(2,1)}, u32[]{:S(2)}) copy-start(bf16[1024,512]{1,0:T(8,128)(2,1)} %param.19) | copy-start | bytes 3145732
  12.6 20.7 %all-to-all-start = ((s32[64,1,32]{2,1,0:T(1,128)}), s32[64,1,32]{2,1,0:T(1,128)S(1)}, u32[]{:S(2)}, u32[]{:S(2)}) async-start(s32[64,1,32]{2,1,0:T(1,128)} %bitcast.1), calls=%async_computation | async-start | bytes 65536 | tf_op jit(solution)/shard_map/all_to_all | solution.py:70
  33.3 6.8 %copy-start.8 = (s32[64,32]{0,1:T(8,128)S(1)}, s32[64,32]{0,1:T(8,128)}, u32[]{:S(2)}) copy-start(s32[64,32]{0,1:T(8,128)} %param.32) | copy-start | bytes 24580
  33.3 6.9 %copy-start.3 = (bf16[1024,512]{1,0:T(8,128)(2,1)S(1)}, bf16[1024,512]{1,0:T(8,128)(2,1)}, u32[]{:S(2)}) copy-start(bf16[1024,512]{1,0:T(8,128)(2,1)} %param.24) | copy-start | bytes 3145732
  33.3 57.8 %all-to-all-start.1 = ((bf16[64,32,512]{2,1,0:T(8,128)(2,1)}), bf16[64,32,512]{2,1,0:T(8,128)(2,1)}, u32[]{:S(2)}, u32[]{:S(2)}) async-start(bf16[64,32,512]{2,1,0:T(8,128)(2,1)} %bitcast.51), calls=%async_computation.1 | async-start | bytes 4194304 | tf_op jit(solution)/shard_map/all_to_all | solution.py:69
  39.8 1.9 copy-start.13
  39.8 109.6 %all-reduce.2.cloned.1.call-start = ((), (), s32[]{:S(2)}) async-start(), calls=%async_computation.4 | async-start | bytes 1048576 | tf_op jit(solution)/shard_map/psum | solution.py:87
  45.6 45.5 %copy-start.5 = (bf16[512,512]{1,0:T(8,128)(2,1)S(1)}, bf16[512,512]{1,0:T(8,128)(2,1)}, u32[]{:S(2)}) copy-start(bf16[512,512]{1,0:T(8,128)(2,1)} %param.23) | copy-start | bytes 1572868
  91.1 4.8 %copy-start.16 = (f32[512]{0:T(512)S(1)}, f32[512]{0:T(512)}, u32[]{:S(2)}) copy-start(f32[512]{0:T(512)} %param.25) | copy-start | bytes 6148
  95.9 6.0 %copy-start.1 = (bf16[512,1024]{1,0:T(8,128)(2,1)S(1)}, bf16[512,1024]{1,0:T(8,128)(2,1)}, u32[]{:S(2)}) copy-start(bf16[512,1024]{1,0:T(8,128)(2,1)} %param.26) | copy-start | bytes 3145732
  101.9 1.6 copy-start.2
  103.5 45.9 %copy-start.14 = (f32[1024]{0:T(1024)S(1)}, f32[1024]{0:T(1024)}, u32[]{:S(2)}) copy-start(f32[1024]{0:T(1024)} %param.27) | copy-start | bytes 12292
  103.5 45.9 %copy-start.15 = (f32[3,256]{1,0:T(4,128)S(1)}, f32[3,256]{1,0:T(4,128)}, u32[]{:S(2)}) copy-start(f32[3,256]{1,0:T(4,128)} %param.30) | copy-start | bytes 9220
  105.1 46.5 %copy-start.4 = (f32[3,256,256]{2,1,0:T(8,128)S(1)}, f32[3,256,256]{2,1,0:T(8,128)}, u32[]{:S(2)}) copy-start(f32[3,256,256]{2,1,0:T(8,128)} %fusion.13) | copy-start | bytes 2359300
  152.7 46.1 %copy-start.6 = (bf16[256,256]{1,0:T(8,128)(2,1)}, bf16[256,256]{1,0:T(8,128)(2,1)S(1)}, u32[]{:S(2)}) copy-start(bf16[256,256]{1,0:T(8,128)(2,1)S(1)} %fusion.50) | copy-start | bytes 393220
  152.7 12.2 %copy-start.9 = (s32[256,10]{0,1:T(8,128)S(1)}, s32[256,10]{0,1:T(8,128)}, u32[]{:S(2)}) copy-start(s32[256,10]{0,1:T(8,128)} %param.33) | copy-start | bytes 30724
  154.3 39.3 %all-to-all-start.2 = ((bf16[64,32,256]{2,1,0:T(8,128)(2,1)}), bf16[64,32,256]{2,1,0:T(8,128)(2,1)S(1)}, u32[]{:S(2)}, u32[]{:S(2)}) async-start(bf16[64,32,256]{2,1,0:T(8,128)(2,1)} %bitcast.53), calls=%async_computation.2 | async-start | bytes 2097152 | tf_op jit(solution)/shard_map/all_to_all | solution.py:106
  164.9 56.5 %reduce-scatter.2.cloned.1.call-start = ((), (), s32[]{:S(2)}) async-start(), calls=%async_computation.5 | async-start | bytes 655360 | tf_op jit(solution)/shard_map/reduce_scatter | solution.py:117
  193.6 5.2 %copy-start.7 = (bf16[256,1024]{1,0:T(8,128)(2,1)S(1)}, bf16[256,1024]{1,0:T(8,128)(2,1)}, u32[]{:S(2)}) copy-start(bf16[256,1024]{1,0:T(8,128)(2,1)} %param.36) | copy-start | bytes 1572868
  193.6 5.2 %copy-start.11 = (s32[256]{0:T(256)S(1)}, s32[256]{0:T(256)}, u32[]{:S(2)}) copy-start(s32[256]{0:T(256)} %param.34) | copy-start | bytes 3076
  198.8 22.5 %copy-start.10 = (f32[1024]{0:T(1024)S(1)}, f32[1024]{0:T(1024)}, u32[]{:S(2)}) copy-start(f32[1024]{0:T(1024)} %param.37) | copy-start | bytes 12292
Sparse Core Ops, SparseCore 0:
  104.9 44.4 all-reduce.1
  201.5 19.8 reduce-scatter.1
where the time goes:
time: 230 us
  waiting for transfers between devices  141 us (61%)
  matrix products  38.1 us (17%)
  starting transfers between devices  29.4 us (13%)
  between operations  14.3 us (6%)
  other arithmetic  5.33 us (2%)
    psum x1, waiting for transfers between devices, per_device(): msg_total = lax.psum(partial_total.astype(BF16), 'mp').astype(F32)  44.3 us
    all_to_all x1, waiting for transfers between devices, per_device(): lax.all_to_all(feat_buffer, 'nodes', split_axis=0, concat_axis=0, tiled=T...  43.1 us
    all_to_all x1, waiting for transfers between devices, per_device(): lax.all_to_all(outgoing, 'nodes', split_axis=0, concat_axis=0, tiled=True)  28.7 us
    reduce_scatter x1, waiting for transfers between devices, per_device(): lax.psum_scatter((jnp.dot(neigh_mean, w_neigh, preferred_element_type=F32...  20 us
    all_to_all x1, starting transfers between devices, per_device(): lax.all_to_all(id_buffer, 'nodes', split_axis=0, concat_axis=0, tiled=True)  12.1 us
    all_to_all x1, starting transfers between devices, per_device(): lax.all_to_all(outgoing, 'nodes', split_axis=0, concat_axis=0, tiled=True)  10.6 us
    all_to_all x1, starting transfers between devices, per_device(): lax.all_to_all(feat_buffer, 'nodes', split_axis=0, concat_axis=0, tiled=T...  6.52 us
    dot_general x1, matrix products, per_device(): hidden_sum = jnp.dot(seg, hidden_msg, preferred_element_type=F32)  5.99 us
  transfers between devices with their start and end apart: 5, of which 5 were waited for; matrix products, arithmetic and copies ran while one was open for 5% of the time, Pallas kernels for 0%

commit v1 on v0

--- a/solution.py
+++ b/solution.py
@@ -1,10 +1,19 @@
+import functools
 import jax
 import jax.numpy as jnp
 from jax import lax
 from jax.sharding import PartitionSpec as P
+from jax.lax import all_gather
 
 F32 = jnp.float32
 BF16 = jnp.bfloat16
+
+
+def _switch_masks(in_array, row_axis):
+    return jnp.sum(all_gather(in_array, row_axis), axis=0)
+
+
+supply_all_area_on = functools.partial(_switch_masks, row_axis="mp")
 
 
 def one_hot(index, size, dtype=BF16):
@@ -84,7 +93,7 @@
     hidden_sum = jnp.dot(seg, hidden_msg, preferred_element_type=F32)
     partial_total = split_dot(hidden_sum, w_msg_out)
     divisor = jnp.maximum(counts, 1.0)[:, None]
-    msg_total = lax.psum(partial_total.astype(BF16), "mp").astype(F32)
+    msg_total = supply_all_area_on(partial_total.astype(BF16)).astype(F32)
     aggregate = (msg_total / divisor + b_out).astype(BF16)
     gates_in = (
         jnp.einsum("nd,gdc->gnc", aggregate, w_input, preferred_element_type=F32)

time: 230 us -> 217 us (0.943)
  waiting for transfers between devices: 141 us -> 127 us
    psum x1 -> x0, waiting for transfers between devices: 44.3 us -> none  [per_device(): msg_total = lax.psum(partial_total.astype(BF16), 'mp').astype(F32)]
    all_gather x0 -> x1, waiting for transfers between devices: none -> 28.6 us  [_switch_masks(): return jnp.sum(all_gather(in_array, row_axis), axis=0)]
    reduce_sum x0 -> x1, other arithmetic: none -> 2.94 us  [_switch_masks(): return jnp.sum(all_gather(in_array, row_axis), axis=0)]
    all_to_all x1, waiting for transfers between devices: 43.1 us -> 45.8 us  [per_device(): lax.all_to_all(feat_buffer, 'nodes', split_axis=0, concat_axis=0, tiled=T...]
where the time goes in v1:
time: 217 us; the launch traced here: 216 us
  waiting for transfers between devices  127 us (59%)
  matrix products  36.1 us (17%)
  starting transfers between devices  29.4 us (14%)
  between operations  14.3 us (7%)
  other arithmetic  7.36 us (3%)
    all_to_all x1, waiting for transfers between devices, per_device(): lax.all_to_all(feat_buffer, 'nodes', split_axis=0, concat_axis=0, tiled=T...  45.8 us
    all_to_all x1, waiting for transfers between devices, per_device(): lax.all_to_all(outgoing, 'nodes', split_axis=0, concat_axis=0, tiled=True)  28.7 us
    all_gather x1, waiting for transfers between devices, _switch_masks(): return jnp.sum(all_gather(in_array, row_axis), axis=0)  28.6 us
    reduce_scatter x1, waiting for transfers between devices, per_device(): lax.psum_scatter((jnp.dot(neigh_mean, w_neigh, preferred_element_type=F32...  19.5 us
    all_to_all x1, starting transfers between devices, per_device(): lax.all_to_all(id_buffer, 'nodes', split_axis=0, concat_axis=0, tiled=True)  12.1 us
    all_to_all x1, starting transfers between devices, per_device(): lax.all_to_all(outgoing, 'nodes', split_axis=0, concat_axis=0, tiled=True)  10.5 us
    all_to_all x1, starting transfers between devices, per_device(): lax.all_to_all(feat_buffer, 'nodes', split_axis=0, concat_axis=0, tiled=T...  6.52 us
    dot_general x1, matrix products, per_device(): hidden_sum = jnp.dot(seg, hidden_msg, preferred_element_type=F32)  5.99 us
  transfers between devices with their start and end apart: 5, of which 5 were waited for; matrix products, arithmetic and copies ran while one was open for 5% of the time, Pallas kernels for 0%

profile of v1, /device:TPU:8, one launch (start us, length us, event | category | flops | bytes accessed | tf_op | source)
XLA Modules:
  0.0 216.4 jit_solution(16276058005356533700)
XLA Ops:
  7.2 0.8 add_convert_fusion.4
  8.2 1.4 fusion.17
  9.6 0.8 convert_add_fusion
  10.4 1.6 fusion.19
  11.9 0.7 sub.16
  12.6 12.1 %all-to-all-start = ((s32[64,1,32]{2,1,0:T(1,128)}), s32[64,1,32]{2,1,0:T(1,128)S(1)}, u32[]{:S(2)}, u32[]{:S(2)}) async-start(s32[64,1,32]{2,1,0:T(1,128)} %bitcast.1), calls=%async_computation | async-start | bytes 65536 | tf_op jit(solution)/shard_map/all_to_all | solution.py:79
  24.7 3.7 %fusion.5 = bf16[2048,512]{1,0:T(8,128)(2,1)} fusion(bf16[1024,512]{1,0:T(8,128)(2,1)S(1)} %copy-done.12, s32[1024]{0:T(1024)S(1)} %convert_add_fusion), kind=kOutput, calls=%fused_computation.8 | convolution fusion | flops 2150629376 | bytes 3149824 | tf_op jit(solution)/shard_map/dot_general | solution.py:73
  28.4 4.9 %all-to-all-done = s32[64,1,32]{2,1,0:T(1,128)S(1)} async-done(((s32[64,1,32]{2,1,0:T(1,128)}), s32[64,1,32]{2,1,0:T(1,128)S(1)}, u32[]{:S(2)}, u32[]{:S(2)}) %all-to-all-start) | async-done | bytes 8224 | tf_op jit(solution)/shard_map/all_to_all | solution.py:79
  33.3 6.5 %all-to-all-start.1 = ((bf16[64,32,512]{2,1,0:T(8,128)(2,1)}), bf16[64,32,512]{2,1,0:T(8,128)(2,1)}, u32[]{:S(2)}, u32[]{:S(2)}) async-start(bf16[64,32,512]{2,1,0:T(8,128)(2,1)} %bitcast.53), calls=%async_computation.1 | async-start | bytes 4194304 | tf_op jit(solution)/shard_map/all_to_all | solution.py:78
  39.8 0.2 all-gather.3.cloned.1.call-start
  40.1 1.5 fusion.78
  41.5 0.5 broadcast.59
  42.1 0.7 reduce.8
  42.9 2.4 %fusion.8 = f32[2048,512]{1,0:T(8,128)} fusion(s32[2048]{0:T(1024)S(1)} %eq.239, f32[256,512]{1,0:T(8,128)S(1)} %fusion.78), kind=kOutput, calls=%fused_computation.25 | convolution fusion | flops 537526272 | bytes 4726784 | tf_op jit(solution)/shard_map/dot_general | solution.py:88
  45.3 45.8 %all-to-all-done.1 = bf16[64,32,512]{2,1,0:T(8,128)(2,1)} async-done(((bf16[64,32,512]{2,1,0:T(8,128)(2,1)}), bf16[64,32,512]{2,1,0:T(8,128)(2,1)}, u32[]{:S(2)}, u32[]{:S(2)}) %all-to-all-start.1) | async-done | bytes 2097184 | tf_op jit(solution)/shard_map/all_to_all | solution.py:78
  91.1 4.8 %fusion.77 = f32[2048,512]{1,0:T(8,128)} fusion(bf16[2048,512]{1,0:T(8,128)(2,1)} %bitcast.3, bf16[512,512]{1,0:T(8,128)(2,1)S(1)} %copy-done.5), kind=kOutput, calls=%fused_computation.104 | convolution fusion | flops 1073741824 | bytes 6815744 | tf_op jit(solution)/shard_map/dot_general | solution.py:91
  95.9 6.0 %fusion.9 = f32[256,512]{1,0:T(8,128)} fusion(s32[2048]{0:T(1024)S(1)} %eq.239, f32[2048,512]{1,0:T(8,128)} %fusion.77, f32[2048,512]{1,0:T(8,128)} %fusion.8, f32[512]{0:T(512)S(1)} %copy-done.16, f32[256,512]{1,0:T(8,128)S(1)} %fusion.78), kind=kOutput, calls=%fused_computation.28 | convolution fusion | flops 1080557568 | bytes 9447424 | tf_op jit(solution)/shard_map/dot_general | solution.py:93
  101.9 1.5 fusion.68
  103.5 1.3 fusion.11
  105.0 0.6 fusion.13
  105.6 0.3 convert_reduce_fusion
  105.9 28.6 %all-gather.3.cloned.1.call-done = bf16[1024,1024]{1,0:T(8,128)(2,1)} async-done(((bf16[256,1024]{1,0:T(8,128)(2,1)}), bf16[1024,1024]{1,0:T(8,128)(2,1)}) %all-gather.3.cloned.1.call-update) | async-done | bytes 2097168 | tf_op jit(solution)/shard_map/all_gather | solution.py:13
  134.4 2.9 %reduce_sum.32 = bf16[256,1024]{1,0:T(8,128)(2,1)} reduce(bf16[4,256,1024]{2,1,0:T(8,128)(2,1)} %bitcast.52, bf16[]{:T(256)} %constant.7.clone.1), dimensions={0}, to_apply=%region_2.3 | reduce | flops 786432 | bytes 2621442 | tf_op jit(solution)/shard_map/reduce_sum | solution.py:13
  137.4 2.2 %fusion.14 = f32[3,256,256]{2,1,0:T(8,128)S(1)} fusion(bf16[3,1024,256]{2,1,0:T(8,128)(2,1)} %param.28, bf16[256,1024]{1,0:T(8,128)(2,1)} %reduce_sum.32, f32[1024]{0:T(1024)S(1)} %copy-done.14, f32[256]{0:T(256)S(1)} %broadcast_maximum_fusion, f32[3,256]{1,0:T(4,128)S(1)} %copy-done.15), kind=kOutput, calls=%fused_computation.37 | convolution fusion | flops 403898368 | bytes 2891776 | tf_op jit(solution)/shard_map/nd,gdc->gnc/dot_general | solution.py:99
  139.6 0.2 fusion.50
  139.8 1.5 convolution_convert_fusion
  141.4 10.5 %all-to-all-start.2 = ((bf16[64,32,256]{2,1,0:T(8,128)(2,1)}), bf16[64,32,256]{2,1,0:T(8,128)(2,1)S(1)}, u32[]{:S(2)}, u32[]{:S(2)}) async-start(bf16[64,32,256]{2,1,0:T(8,128)(2,1)} %bitcast.55), calls=%async_computation.2 | async-start | bytes 2097152 | tf_op jit(solution)/shard_map/all_to_all | solution.py:115
  152.0 28.7 %all-to-all-done.2 = bf16[64,32,256]{2,1,0:T(8,128)(2,1)S(1)} async-done(((bf16[64,32,256]{2,1,0:T(8,128)(2,1)}), bf16[64,32,256]{2,1,0:T(8,128)(2,1)S(1)}, u32[]{:S(2)}, u32[]{:S(2)}) %all-to-all-start.2) | async-done | bytes 1048608 | tf_op jit(solution)/shard_map/all_to_all | solution.py:115
  180.7 5.2 %fusion.18 = f32[256,1024]{1,0:T(8,128)} fusion(bf16[256,1024]{1,0:T(8,128)(2,1)} %param.35, bf16[2048,256]{1,0:T(8,128)(2,1)S(1)} %bitcast.54, s32[256]{0:T(256)S(1)} %bitcast.66, s32[256]{0:T(256)S(1)} %bitcast.67, s32[256]{0:T(256)S(1)} %bitcast.59, s32[256]{0:T(256)S(1)} %bitcast.60, s32[256]{0:T(256)S(1)} %bitcast.61, s32[256]{0:T(256)S(1)} %bitcast.62, ...), kind=kOutput, calls=%fused_computation.43 | convolution fusion | flops 418512896 | bytes 2631680 | tf_op jit(solution)/shard_map/dot_general | solution.py:128
  185.9 2.5 %fusion.12 = bf16[256,1024]{1,0:T(8,128)(2,1)} fusion(f32[256,1024]{1,0:T(8,128)} %fusion.18, bf16[256,1024]{1,0:T(8,128)(2,1)S(1)} %copy-done.7, bf16[256,256]{1,0:T(8,128)(2,1)S(1)} %fusion.50, s32[256]{0:T(256)S(1)} %copy-done.11), kind=kOutput, calls=%fused_computation.33 | convolution fusion | flops 168427520 | bytes 2229248 | tf_op jit(solution)/shard_map/dot_general | solution.py:129
  188.5 19.5 %reduce-scatter.2.cloned.1.call-done = bf16[64,1024]{1,0:T(8,128)(2,1)} async-done(((bf16[256,1024]{1,0:T(8,128)(2,1)}), bf16[64,1024]{1,0:T(8,128)(2,1)}) %reduce-scatter.2.cloned.1.call-update) | async-done | bytes 131088 | tf_op jit(solution)/shard_map/reduce_scatter | solution.py:126
  207.9 1.6 maximum_convert_fusion.1
  (44 shorter events, 0.6 us)
Async XLA Ops:
  7.2 97.8 %copy-start = (bf16[3,1024,256]{2,1,0:T(8,128)(2,1)S(1)}, bf16[3,1024,256]{2,1,0:T(8,128)(2,1)}, u32[]{:S(2)}) copy-start(bf16[3,1024,256]{2,1,0:T(8,128)(2,1)} %param.29) | copy-start | bytes 4718596
  9.6 15.2 %copy-start.12 = (bf16[1024,512]{1,0:T(8,128)(2,1)S(1)}, bf16[1024,512]{1,0:T(8,128)(2,1)}, u32[]{:S(2)}) copy-start(bf16[1024,512]{1,0:T(8,128)(2,1)} %param.19) | copy-start | bytes 3145732
  12.6 20.7 %all-to-all-start = ((s32[64,1,32]{2,1,0:T(1,128)}), s32[64,1,32]{2,1,0:T(1,128)S(1)}, u32[]{:S(2)}, u32[]{:S(2)}) async-start(s32[64,1,32]{2,1,0:T(1,128)} %bitcast.1), calls=%async_computation | async-start | bytes 65536 | tf_op jit(solution)/shard_map/all_to_all | solution.py:79
  33.3 6.8 %copy-start.3 = (bf16[1024,512]{1,0:T(8,128)(2,1)S(1)}, bf16[1024,512]{1,0:T(8,128)(2,1)}, u32[]{:S(2)}) copy-start(bf16[1024,512]{1,0:T(8,128)(2,1)} %param.24) | copy-start | bytes 3145732
  33.3 57.8 %all-to-all-start.1 = ((bf16[64,32,512]{2,1,0:T(8,128)(2,1)}), bf16[64,32,512]{2,1,0:T(8,128)(2,1)}, u32[]{:S(2)}, u32[]{:S(2)}) async-start(bf16[64,32,512]{2,1,0:T(8,128)(2,1)} %bitcast.53), calls=%async_computation.1 | async-start | bytes 4194304 | tf_op jit(solution)/shard_map/all_to_all | solution.py:78
  39.8 94.6 %all-gather.3.cloned.1.call-start = ((), (), s32[]{:S(2)}) async-start(), calls=%async_computation.5 | async-start | bytes 2621440 | tf_op jit(solution)/shard_map/all_gather | solution.py:13
  42.9 48.2 %copy-start.5 = (bf16[512,512]{1,0:T(8,128)(2,1)S(1)}, bf16[512,512]{1,0:T(8,128)(2,1)}, u32[]{:S(2)}) copy-start(bf16[512,512]{1,0:T(8,128)(2,1)} %param.23) | copy-start | bytes 1572868
  91.1 4.8 %copy-start.16 = (f32[512]{0:T(512)S(1)}, f32[512]{0:T(512)}, u32[]{:S(2)}) copy-start(f32[512]{0:T(512)} %param.25) | copy-start | bytes 6148
  95.9 6.0 %copy-start.1 = (bf16[512,1024]{1,0:T(8,128)(2,1)S(1)}, bf16[512,1024]{1,0:T(8,128)(2,1)}, u32[]{:S(2)}) copy-start(bf16[512,1024]{1,0:T(8,128)(2,1)} %param.26) | copy-start | bytes 3145732
  101.9 1.6 copy-start.2
  103.5 1.3 copy-start.8
  103.5 1.5 copy-start.4
  103.5 1.5 copy-start.13
  105.0 32.4 %copy-start.14 = (f32[1024]{0:T(1024)S(1)}, f32[1024]{0:T(1024)}, u32[]{:S(2)}) copy-start(f32[1024]{0:T(1024)} %param.27) | copy-start | bytes 12292
  105.0 32.4 %copy-start.15 = (f32[3,256]{1,0:T(4,128)S(1)}, f32[3,256]{1,0:T(4,128)}, u32[]{:S(2)}) copy-start(f32[3,256]{1,0:T(4,128)} %param.30) | copy-start | bytes 9220
  139.8 46.1 %copy-start.6 = (bf16[256,256]{1,0:T(8,128)(2,1)}, bf16[256,256]{1,0:T(8,128)(2,1)S(1)}, u32[]{:S(2)}) copy-start(bf16[256,256]{1,0:T(8,128)(2,1)S(1)} %fusion.50) | copy-start | bytes 393220
  139.8 12.2 %copy-start.9 = (s32[256,10]{0,1:T(8,128)S(1)}, s32[256,10]{0,1:T(8,128)}, u32[]{:S(2)}) copy-start(s32[256,10]{0,1:T(8,128)} %param.33) | copy-start | bytes 30724
  141.4 39.3 %all-to-all-start.2 = ((bf16[64,32,256]{2,1,0:T(8,128)(2,1)}), bf16[64,32,256]{2,1,0:T(8,128)(2,1)S(1)}, u32[]{:S(2)}, u32[]{:S(2)}) async-start(bf16[64,32,256]{2,1,0:T(8,128)(2,1)} %bitcast.55), calls=%async_computation.2 | async-start | bytes 2097152 | tf_op jit(solution)/shard_map/all_to_all | solution.py:115
  151.9 56.0 %reduce-scatter.2.cloned.1.call-start = ((), (), s32[]{:S(2)}) async-start(), calls=%async_computation.4 | async-start | bytes 655360 | tf_op jit(solution)/shard_map/reduce_scatter | solution.py:126
  180.7 5.2 %copy-start.7 = (bf16[256,1024]{1,0:T(8,128)(2,1)S(1)}, bf16[256,1024]{1,0:T(8,128)(2,1)}, u32[]{:S(2)}) copy-start(bf16[256,1024]{1,0:T(8,128)(2,1)} %param.36) | copy-start | bytes 1572868
  180.7 5.2 %copy-start.11 = (s32[256]{0:T(256)S(1)}, s32[256]{0:T(256)}, u32[]{:S(2)}) copy-start(s32[256]{0:T(256)} %param.34) | copy-start | bytes 3076
  185.9 22.0 %copy-start.10 = (f32[1024]{0:T(1024)S(1)}, f32[1024]{0:T(1024)}, u32[]{:S(2)}) copy-start(f32[1024]{0:T(1024)} %param.37) | copy-start | bytes 12292
Sparse Core Ops, SparseCore 0:
  104.9 29.4 all-gather.2
  188.6 19.3 reduce-scatter.1
